TPU v7x, 32 devices: a whole 2x2x4 slice. The times are simulated.
32 devices in a mesh: tm: 8 (over z, y), cal: 4 (over x, core).
Axes of the slice: x: 2, y: 2, z: 4, core: 2. Of those that a mesh axis runs over, the one named last changes fastest.
Arguments:
- src_design: float32 [5, 4096, 128], P(None, ('tm', 'cal')), may hold values from -6 to 6
- att_design: float32 [3, 4096, 128], P(None, ('tm', 'cal')), may hold values from -6 to 6
- obs_phase: float32 [4096, 128], P(('tm', 'cal')), may hold values from 0 to 1
- cal_design: float32 [4096, 128], P(('tm', 'cal')), may hold values from -6 to 6
- obs_weight: float32 [4096, 128], P(('tm', 'cal')), may hold values from 0.1 to 12
- knot_index: int32 [4096, 128], P(('tm', 'cal')), may hold values from 0 to 4092, as said below
- cal_block: int32 [4096, 128], P(('tm', 'cal')), may hold values from 0 to 7
- cal_column: int32 [4096, 128], P(('tm', 'cal')), may hold values from 0 to 4095
- obs_count: int32 [4096], P(('tm', 'cal')), may hold values from 32 to 128
- src_res: float32 [5, 4096], P(None, ('tm', 'cal')), may hold values from -6 to 6
- att_res: float32 [3, 4096], P(None, ('tm', 'cal')), may hold values from -6 to 6
- cal_res: float32 [8, 4096], P('cal'), may hold values from -6 to 6
- src_dir: float32 [5, 4096], P(None, ('tm', 'cal')), may hold values from -6 to 6
- att_dir: float32 [3, 4096], P(None, ('tm', 'cal')), may hold values from -6 to 6
- cal_dir: float32 [8, 4096], P('cal'), may hold values from -6 to 6
Outputs:
- new_src_res: float32 [5, 4096], P(None, ('tm', 'cal'))
- new_att_res: float32 [3, 4096], P(None, ('tm', 'cal'))
- new_cal_res: float32 [8, 4096], P('cal')
- new_src_dir: float32 [5, 4096], P(None, ('tm', 'cal'))
- new_att_dir: float32 [3, 4096], P(None, ('tm', 'cal'))
- new_cal_dir: float32 [8, 4096], P('cal')
Inputs may be any that keep to these rules, and one draw needn't show every extreme that they name: The observations of source row s have knot intervals from (s // 128) * 128 to (s // 128) * 128 + 127, and knot_index + 3 < 4096.
All inputs are finite; a program needn't handle non-finite values.
Results may differ from a plain program's by a relative error of at most 0.00015.
Values sent between devices are 32-bit elements; how exact they have to be, the bound alone decides.
No kernel may reach another device: no remote copies, remote signals or barrier semaphores. Data moves between devices by JAX's collectives and lax.ppermute only.
A program may use at most 64 MiB of HBM per device.

v0:
```python
import math
import jax
import jax.numpy as jnp
from jax import lax
from jax.sharding import PartitionSpec as P


def passed_along(block, axis, distance):
    devices = range(lax.axis_size(axis))
    route = [(i - distance, i) for i in devices if i - distance in devices]
    return lax.ppermute(block, axis, route)


def spline(phase):
    rest = 1.0 - phase
    cube = phase * phase * phase
    square = phase * phase
    first = rest * rest * rest / 6.0
    second = (3.0 * cube - 6.0 * square + 4.0) / 6.0
    third = (-3.0 * cube + 3.0 * square + 3.0 * phase + 1.0) / 6.0
    fourth = cube / 6.0
    return (first, second, third, fourth)


def local(
    src_design,
    att_design,
    obs_phase,
    cal_design,
    obs_weight,
    knot_index,
    cal_block,
    cal_column,
    obs_count,
    src_res,
    att_res,
    cal_res,
    src_dir,
    att_dir,
    cal_dir,
):
    knot_count = att_dir.shape[1]
    extended = knot_count + 3
    blocks, col_width = cal_dir.shape
    all_blocks = blocks * lax.axis_size("cal")
    src_rows, slots = obs_phase.shape
    group = math.gcd(src_rows, 16)
    group_count = src_rows // group
    first_row = (lax.axis_index("tm") == 0).astype(jnp.float32)
    cal_values = lax.all_gather(cal_dir, "cal", axis=0, tiled=True)
    edge_knots = passed_along(att_dir[:, :3], ("tm", "cal"), -1)
    att_ext = jnp.concatenate([att_dir, edge_knots], axis=1)
    live_mask = (lax.broadcasted_iota(jnp.int32, obs_phase.shape, 1) < obs_count[:, None]).astype(
        jnp.float32
    )
    local_knot = knot_index - lax.axis_index(("tm", "cal")) * knot_count
    knot_iota = lax.broadcasted_iota(jnp.int32, (1, 1, extended), 2)

    def block_inputs(which):
        start = which * group
        knots = lax.dynamic_slice_in_dim(local_knot, start, group, 0)
        design = lax.dynamic_slice_in_dim(att_design, start, group, 1)
        phases = lax.dynamic_slice_in_dim(obs_phase, start, group, 0)
        return (start, knots, design, spline(phases))

    def forward(which):
        start, knots, design, weights = block_inputs(which)
        total = jnp.zeros((group, slots), jnp.float32)
        for offset in range(4):
            onehot = ((knots + offset)[:, :, None] == knot_iota).astype(jnp.float32)
            picked = jnp.einsum("bok,ck->cbo", onehot, att_ext, precision=lax.Precision.HIGHEST)
            total = total + weights[offset] * jnp.sum(design * picked, axis=0)
        return total

    y_att = lax.map(forward, jnp.arange(group_count, dtype=jnp.int32)).reshape(src_rows, slots)
    y_src = jnp.sum(src_design * src_dir[:, :, None], axis=0)
    flat_index = cal_block * col_width + cal_column
    y_cal = cal_design * jnp.take(cal_values.reshape(-1), flat_index)
    response = live_mask * (y_src + y_att + y_cal)
    weighted = obs_weight * response
    curv_local = jnp.sum(weighted * response)
    norm_local = (
        jnp.sum(src_res * src_res)
        + jnp.sum(att_res * att_res)
        + first_row * jnp.sum(cal_res * cal_res)
    )
    cal_term = jax.ops.segment_sum(
        (cal_design * weighted).reshape(-1),
        flat_index.reshape(-1),
        num_segments=all_blocks * col_width,
    ).reshape(all_blocks, col_width)
    q_src = jnp.sum(src_design * weighted[None], axis=2)

    def backward(which, grad_sum):
        start, knots, design, weights = block_inputs(which)
        scaled = design * lax.dynamic_slice_in_dim(weighted, start, group, 0)[None]
        for offset in range(4):
            onehot = ((knots + offset)[:, :, None] == knot_iota).astype(jnp.float32)
            grad_sum = grad_sum + jnp.einsum(
                "cbo,bok->ck",
                weights[offset][None] * scaled,
                onehot,
                precision=lax.Precision.HIGHEST,
            )
        return grad_sum

    grad_ext = lax.fori_loop(0, group_count, backward, jnp.zeros((3, extended), jnp.float32))
    incoming = passed_along(grad_ext[:, knot_count:], ("tm", "cal"), 1)
    q_att = jnp.concatenate([grad_ext[:, :3] + incoming, grad_ext[:, 3:knot_count]], axis=1)
    norm_now, curvature = lax.psum((norm_local, curv_local), ("tm", "cal"))
    shared = lax.psum_scatter(cal_term, "cal", scatter_dimension=0, tiled=True)
    q_cal = lax.psum(shared, "tm")
    step_len = norm_now / curvature
    new_src_res = src_res - step_len * q_src
    new_att_res = att_res - step_len * q_att
    new_cal_res = cal_res - step_len * q_cal
    next_local = (
        jnp.sum(new_src_res * new_src_res)
        + jnp.sum(new_att_res * new_att_res)
        + first_row * jnp.sum(new_cal_res * new_cal_res)
    )
    norm_next = lax.psum(next_local, ("tm", "cal"))
    ratio = norm_next / norm_now
    return (
        new_src_res,
        new_att_res,
        new_cal_res,
        new_src_res + ratio * src_dir,
        new_att_res + ratio * att_dir,
        new_cal_res + ratio * cal_dir,
    )


def solution(mesh):
    return jax.shard_map(
        local,
        mesh=mesh,
        in_specs=(
            P(None, ("tm", "cal"), None),
            P(None, ("tm", "cal"), None),
            P(("tm", "cal"), None),
            P(("tm", "cal"), None),
            P(("tm", "cal"), None),
            P(("tm", "cal"), None),
            P(("tm", "cal"), None),
            P(("tm", "cal"), None),
            P(("tm", "cal")),
            P(None, ("tm", "cal")),
            P(None, ("tm", "cal")),
            P("cal", None),
            P(None, ("tm", "cal")),
            P(None, ("tm", "cal")),
            P("cal", None),
        ),
        out_specs=(
            P(None, ("tm", "cal")),
            P(None, ("tm", "cal")),
            P("cal", None),
            P(None, ("tm", "cal")),
            P(None, ("tm", "cal")),
            P("cal", None),
        ),
        check_vma=False,
    )
```

profile of v0, /device:TPU:14, one launch (start us, length us, event | category | flops | bytes accessed | tf_op | source)
XLA Modules:
  0.0 395.8 jit_solution(5462069088811584754)
XLA Ops:
  7.2 1.9 collective-permute-start
  9.2 0.9 bitcast_clamp_fusion
  10.1 0.9 fusion.84
  11.0 5.4 %all-gather = f32[4,2,4096]{2,1,0:T(2,128)S(1)} all-gather(f32[1,2,4096]{2,1,0:T(2,128)S(1)} %bitcast.109), channel_id=1, replica_groups=mesh['tm'=8,'cal'=4] {'cal'}, dimensions={0}, use_global_device_ids=true | all-gather | bytes 163840 | tf_op jit(solution)/shard_map/all_gather | solution.py:50
  18.3 0.6 multiply_reduce_fusion.4
  19.0 90.5 %gather_fusion = f32[16384]{0:T(1024)S(1)} fusion(f32[32768]{0:T(1024)S(1)} %bitcast.107, s32[16384]{0:T(1024)S(1)} %bitcast_clamp_fusion), kind=kCustom, calls=%fused_computation | custom fusion | bytes 196608 | tf_op jit(solution)/shard_map/jit(_take)/gather | solution.py:78
  109.7 0.6 copy-done.9
  113.7 31.6 %while.27 = (s32[]{:T(128)}, f32[8,16,128]{2,1,0:T(8,128)S(1)}, s32[8]{0:T(128)S(1)}, f32[128,128]{1,0:T(8,128)}, f32[3,128,128]{2,0,1:T(4,128)S(1)}, /*index=5*...) while((s32[]{:T(128)}, f32[8,16,128]{2,1,0:T(8,128)S(1)}, ...), condition=%wide.region_10.11_spmd.clone.clone, body=%wide.region_5.10_spmd.clone.clone.sunk | while | flops 39806980 | bytes 268635 | solution.py:75
  116.9 0.7 fusion.113
  120.9 0.7 fusion.113
  124.8 0.7 fusion.113
  128.8 0.7 fusion.113
  132.7 0.7 fusion.113
  136.7 0.7 fusion.113
  140.6 0.7 fusion.113
  144.6 0.7 fusion.113
  145.6 26.0 %while.28 = (s32[]{:T(128)}, f32[3,131]{1,0:T(4,128)S(1)}, f32[128,128]{1,0:T(8,128)}, f32[3,128,128]{2,0,1:T(4,128)S(1)}, f32[128,128]{1,0:T(8,128)S(1)}, /*ind...) while((s32[]{:T(128)}, f32[3,131]{1,0:T(4,128)S(1)}, ...), condition=%wide.region_15.16_spmd.clone.clone, body=%wide.region_14.15_spmd.clone.clone.sunk | while | flops 39802800 | bytes 358733 | solution.py:107
  145.7 0.7 fusion.118
  147.6 0.6 fusion.121
  148.2 0.6 fusion.122
  148.9 0.7 fusion.118
  150.9 0.6 fusion.121
  151.5 0.6 fusion.122
  152.2 0.7 fusion.118
  154.1 0.6 fusion.121
  154.7 0.6 fusion.122
  155.4 0.7 fusion.118
  157.4 0.6 fusion.121
  158.0 0.6 fusion.122
  158.7 0.7 fusion.118
  160.6 0.6 fusion.121
  161.3 0.6 fusion.122
  162.0 0.7 fusion.118
  164.5 0.6 fusion.122
  165.2 0.7 fusion.118
  167.8 0.6 fusion.122
  168.5 0.7 fusion.118
  171.0 0.6 fusion.122
  172.4 2.2 collective-permute-start.1
  174.6 85.9 %scatter_custom_fusion = f32[32768]{0:T(1024)S(1)} fusion(s32[16384]{0:T(1024)S(1)} %fusion.84, f32[16384]{0:T(1024)S(1)} %get-tuple-element.350, f32[]{:T(128)} %constant.148.clone.1), kind=kCustom, calls=%fused_computation.114 | custom fusion | flops 16384 | bytes 131076 | tf_op jit(solution)/shard_map/scatter-add | solution.py:87
  260.5 0.7 reshape.50
  261.2 41.9 %all-reduce.1 = (f32[]{:T(128)}, f32[]{:T(128)}) all-reduce(f32[]{:T(128)S(6)} %add.198, f32[]{:T(128)} %multiply_reduce_fusion.2), channel_id=1, replica_groups=mesh['tm'=8,'cal'=4] {'tm','cal'}, use_global_device_ids=true, to_apply=%region_3.0 | all-reduce | flops 2 | bytes 16 | tf_op jit(solution)/shard_map/psum | solution.py:110
  305.1 0.7 multiply_reduce_fusion.7
  307.1 0.9 constant_dynamic-slice_fusion.3
  308.0 30.1 %psum.30 = f32[2,4096]{1,0:T(2,128)S(1)} all-reduce(f32[2,4096]{1,0:T(2,128)S(1)} %constant_dynamic-slice_fusion.3), channel_id=1, replica_groups=mesh['tm'=8,'cal'=4] {'tm'}, use_global_device_ids=true, to_apply=%region_18.19 | all-reduce | flops 8192 | bytes 65536 | tf_op jit(solution)/shard_map/psum | solution.py:112
  338.1 0.6 multiply_reduce_fusion.3
  339.4 46.4 %psum.31 = f32[]{:T(128)} all-reduce(f32[]{:T(128)S(6)} %add.207), channel_id=1, replica_groups=mesh['tm'=8,'cal'=4] {'tm','cal'}, use_global_device_ids=true, to_apply=%region_22.23 | all-reduce | flops 1 | bytes 8 | tf_op jit(solution)/shard_map/psum | solution.py:122
  388.4 0.6 multiply_add_fusion.1
  (151 shorter events, 37.5 us)
Async XLA Ops:
  7.2 3.9 copy-start.4
  7.2 299.9 %all-reduce.4.cloned.1.call-start = ((), (), s32[]{:S(2)}) async-start(), calls=%async_computation | async-start | bytes 262144
  7.2 106.4 %collective-permute-start = (f32[3,3]{1,0:T(4,128)}, f32[3,3]{1,0:T(4,128)S(1)}, u32[]{:S(2)}, u32[]{:S(2)}) collective-permute-start(f32[3,3]{1,0:T(4,128)} %bitcast.110), channel_id=1, source_target_pairs={{1,0},{2,1},{3,2},{4,3},{5,4},{6,5},{7,6},{8,7},{9,8},{10,9},{11,1... | collective-permute-start | bytes 116 | tf_op jit(solution)/shard_map/ppermute | solution.py:11
  10.1 6.4 %copy-start.3 = (f32[3,128,128]{2,1,0:T(8,128)S(1)}, f32[3,128,128]{2,1,0:T(8,128)}, u32[]{:S(2)}) copy-start(f32[3,128,128]{2,1,0:T(8,128)} %param.20) | copy-start | bytes 589828
  16.5 0.7 copy-start.12
  16.5 1.3 copy-start.13
  16.5 1.9 copy-start.6
  19.0 90.5 %copy-start = (f32[5,128,128]{2,1,0:T(8,128)S(1)}, f32[5,128,128]{2,1,0:T(8,128)}, u32[]{:S(2)}) copy-start(f32[5,128,128]{2,1,0:T(8,128)} %param.19) | copy-start | bytes 983044
  19.0 90.5 %copy-start.10 = (f32[5,128]{1,0:T(8,128)S(1)}, f32[5,128]{1,0:T(8,128)}, u32[]{:S(2)}) copy-start(f32[5,128]{1,0:T(8,128)} %param.31) | copy-start | bytes 7684
  109.5 0.8 copy-start.9
  109.6 2.8 copy-start.17
  109.6 4.0 %copy-start.14 = (f32[3,128]{1,0:T(4,128)S(1)}, f32[3,128]{1,0:T(4,128)}, u32[]{:S(2)}) copy-start(f32[3,128]{1,0:T(4,128)} %param.32) | copy-start | bytes 4612
  113.6 31.7 %copy-start.1 = (s32[128,128]{1,0:T(8,128)S(1)}, s32[128,128]{1,0:T(8,128)}, u32[]{:S(2)}) copy-start(s32[128,128]{1,0:T(8,128)} %param.26) | copy-start | bytes 196612
  113.6 31.7 %copy-start.2 = (s32[128,128]{1,0:T(8,128)S(1)}, s32[128,128]{1,0:T(8,128)}, u32[]{:S(2)}) copy-start(s32[128,128]{1,0:T(8,128)} %param.25) | copy-start | bytes 196612
  113.7 31.7 %copy-start.7 = (f32[128,128]{1,0:T(8,128)S(1)}, f32[128,128]{1,0:T(8,128)}, u32[]{:S(2)}) copy-start(f32[128,128]{1,0:T(8,128)} %param.22) | copy-start | bytes 196612
  113.7 31.7 %copy-start.8 = (f32[128,128]{1,0:T(8,128)S(1)}, f32[128,128]{1,0:T(8,128)}, u32[]{:S(2)}) copy-start(f32[128,128]{1,0:T(8,128)} %param.23) | copy-start | bytes 196612
  113.7 31.7 %copy-start.16 = (s32[128]{0:T(128)S(1)}, s32[128]{0:T(128)}, u32[]{:S(2)}) copy-start(s32[128]{0:T(128)} %param.27) | copy-start | bytes 1540
  172.4 132.7 %collective-permute-start.1 = (f32[3,3]{1,0:T(4,128)S(1)}, f32[3,3]{1,0:T(4,128)S(1)}, u32[]{:S(2)}, u32[]{:S(2)}) collective-permute-start(f32[3,3]{1,0:T(4,128)S(1)} %slice.14), channel_id=1, source_target_pairs={{0,1},{1,2},{2,3},{3,4},{4,5},{5,6},{6,7},{7,8},{8,9},{9,10},{10,1... | collective-permute-start | bytes 116 | tf_op jit(solution)/shard_map/ppermute | solution.py:11
  305.0 84.0 %copy-start.11 = (f32[5,128]{1,0:T(8,128)}, f32[5,128]{1,0:T(8,128)S(1)}, u32[]{:S(2)}) copy-start(f32[5,128]{1,0:T(8,128)S(1)} %get-tuple-element.349) | copy-start | bytes 7684
  305.7 83.3 %copy-start.15 = (f32[3,128]{1,0:T(4,128)}, f32[3,128]{1,0:T(4,128)S(1)}, u32[]{:S(2)}) copy-start(f32[3,128]{1,0:T(4,128)S(1)} %get-tuple-element.347) | copy-start | bytes 4612
  338.8 50.2 %copy-start.5 = (f32[2,4096]{1,0:T(2,128)}, f32[2,4096]{1,0:T(2,128)S(1)}, u32[]{:S(2)}) copy-start(f32[2,4096]{1,0:T(2,128)S(1)} %get-tuple-element.345) | copy-start | bytes 98308
Sparse Core Ops, SparseCore 0:
  261.3 33.1 all-reduce.3
where the time goes:
time: 398 us; the launch traced here: 396 us
  blocking collectives  124 us (31%)
  other arithmetic  106 us (27%)
  local copies, waits for them, and re-layouts  98.9 us (25%)
  matrix products  35.3 us (9%)
  between operations  21.6 us (5%)
  loops' own time  6.01 us (2%)
  starting transfers between devices  4.2 us (1%)
    gather x1, local copies, waits for them, and re-layouts, local(): y_cal = cal_design * jnp.take(cal_values.reshape(-1), flat_index)  90.5 us
    scatter-add x1, other arithmetic, local(): jax.ops.segment_sum((cal_design * weighted).reshape(-1), flat_index.resha...  85.9 us
    psum x1, blocking collectives, local(): norm_next = lax.psum(next_local, ('tm', 'cal'))  46.4 us
    psum x1, blocking collectives, local(): norm_now, curvature = lax.psum((norm_local, curv_local), ('tm', 'cal'))  41.9 us
    psum x1, blocking collectives, local(): q_cal = lax.psum(shared, 'tm')  30.1 us
    dot_general x32, matrix products, backward(): jnp.einsum('cbo,bok->ck', weights[offset][None] * scaled, onehot, precisi...  19.8 us
    dot_general x32, matrix products, forward(): jnp.einsum('bok,ck->cbo', onehot, att_ext, precision=lax.Precision.HIGHEST)  15.4 us
  transfers between devices with their start and end apart: 3, of which 0 were waited for; matrix products, arithmetic and copies ran while one was open for 46% of the time, Pallas kernels for 0%

commit v1 on v0

--- a/solution.py
+++ b/solution.py
@@ -119,7 +119,9 @@
         + jnp.sum(new_att_res * new_att_res)
         + first_row * jnp.sum(new_cal_res * new_cal_res)
     )
-    norm_next = lax.psum(next_local, ("tm", "cal"))
+    norm_next = next_local
+    for mesh_axis in ("cal", "tm"):
+        norm_next = lax.psum(norm_next, mesh_axis)
     ratio = norm_next / norm_now
     return (
         new_src_res,

time: 398 us -> 383 us (0.962)
  blocking collectives: 124 us -> 106 us
    psum x1 -> x2, blocking collectives: 46.4 us -> 29 us  [local(): norm_next = lax.psum(norm_next, mesh_axis)]
  transfers between devices with their start and end apart: 3 -> 3, of which waited for: 0 -> 0; matrix products, arithmetic and copies ran while one was open for 46% -> 48% of each run, Pallas kernels for 0% -> 0%
where the time goes in v1:
time: 383 us; the launch traced here: 378 us
  other arithmetic  106 us (28%)
  blocking collectives  106 us (28%)
  local copies, waits for them, and re-layouts  98.9 us (26%)
  matrix products  35.3 us (9%)
  between operations  21.6 us (6%)
  loops' own time  6.01 us (2%)
  starting transfers between devices  4.2 us (1%)
    gather x1, local copies, waits for them, and re-layouts, local(): y_cal = cal_design * jnp.take(cal_values.reshape(-1), flat_index)  90.5 us
    scatter-add x1, other arithmetic, local(): jax.ops.segment_sum((cal_design * weighted).reshape(-1), flat_index.resha...  85.9 us
    psum x1, blocking collectives, local(): norm_now, curvature = lax.psum((norm_local, curv_local), ('tm', 'cal'))  41.9 us
    psum x1, blocking collectives, local(): q_cal = lax.psum(shared, 'tm')  30.1 us
    psum x2, blocking collectives, local(): norm_next = lax.psum(norm_next, mesh_axis)  29 us
    dot_general x32, matrix products, backward(): jnp.einsum('cbo,bok->ck', weights[offset][None] * scaled, onehot, precisi...  19.8 us
    dot_general x32, matrix products, forward(): jnp.einsum('bok,ck->cbo', onehot, att_ext, precision=lax.Precision.HIGHEST)  15.4 us
  transfers between devices with their start and end apart: 3, of which 0 were waited for; matrix products, arithmetic and copies ran while one was open for 48% of the time, Pallas kernels for 0%

profile of v1, /device:TPU:14, one launch (start us, length us, event | category | flops | bytes accessed | tf_op | source)
XLA Modules:
  0.0 378.4 jit_solution(2400577012744551419)
XLA Ops:
  7.2 1.9 collective-permute-start
  9.2 0.9 bitcast_clamp_fusion
  10.1 0.9 fusion.84
  11.0 5.4 %all-gather = f32[4,2,4096]{2,1,0:T(2,128)S(1)} all-gather(f32[1,2,4096]{2,1,0:T(2,128)S(1)} %bitcast.109), channel_id=1, replica_groups=mesh['tm'=8,'cal'=4] {'cal'}, dimensions={0}, use_global_device_ids=true | all-gather | bytes 163840 | tf_op jit(solution)/shard_map/all_gather | solution.py:50
  18.3 0.6 multiply_reduce_fusion.4
  19.0 90.5 %gather_fusion = f32[16384]{0:T(1024)S(1)} fusion(f32[32768]{0:T(1024)S(1)} %bitcast.107, s32[16384]{0:T(1024)S(1)} %bitcast_clamp_fusion), kind=kCustom, calls=%fused_computation | custom fusion | bytes 196608 | tf_op jit(solution)/shard_map/jit(_take)/gather | solution.py:78
  109.7 0.6 copy-done.9
  113.7 31.6 %while.27 = (s32[]{:T(128)}, f32[8,16,128]{2,1,0:T(8,128)S(1)}, s32[8]{0:T(128)S(1)}, f32[128,128]{1,0:T(8,128)}, f32[3,128,128]{2,0,1:T(4,128)S(1)}, /*index=5*...) while((s32[]{:T(128)}, f32[8,16,128]{2,1,0:T(8,128)S(1)}, ...), condition=%wide.region_10.11_spmd.clone.clone, body=%wide.region_5.10_spmd.clone.clone.sunk | while | flops 39806980 | bytes 268635 | solution.py:75
  116.9 0.7 fusion.113
  120.9 0.7 fusion.113
  124.8 0.7 fusion.113
  128.8 0.7 fusion.113
  132.7 0.7 fusion.113
  136.7 0.7 fusion.113
  140.6 0.7 fusion.113
  144.6 0.7 fusion.113
  145.6 26.0 %while.28 = (s32[]{:T(128)}, f32[3,131]{1,0:T(4,128)S(1)}, f32[128,128]{1,0:T(8,128)}, f32[3,128,128]{2,0,1:T(4,128)S(1)}, f32[128,128]{1,0:T(8,128)S(1)}, /*ind...) while((s32[]{:T(128)}, f32[3,131]{1,0:T(4,128)S(1)}, ...), condition=%wide.region_15.16_spmd.clone.clone, body=%wide.region_14.15_spmd.clone.clone.sunk | while | flops 39802800 | bytes 358733 | solution.py:107
  145.7 0.7 fusion.118
  147.6 0.6 fusion.121
  148.2 0.6 fusion.122
  148.9 0.7 fusion.118
  150.9 0.6 fusion.121
  151.5 0.6 fusion.122
  152.2 0.7 fusion.118
  154.1 0.6 fusion.121
  154.7 0.6 fusion.122
  155.4 0.7 fusion.118
  157.4 0.6 fusion.121
  158.0 0.6 fusion.122
  158.7 0.7 fusion.118
  161.3 0.6 fusion.122
  162.0 0.7 fusion.118
  164.5 0.6 fusion.122
  165.2 0.7 fusion.118
  167.8 0.6 fusion.122
  168.5 0.7 fusion.118
  171.0 0.6 fusion.122
  172.4 2.2 collective-permute-start.1
  174.6 85.9 %scatter_custom_fusion = f32[32768]{0:T(1024)S(1)} fusion(s32[16384]{0:T(1024)S(1)} %fusion.84, f32[16384]{0:T(1024)S(1)} %get-tuple-element.350, f32[]{:T(128)} %constant.148.clone.1), kind=kCustom, calls=%fused_computation.114 | custom fusion | flops 16384 | bytes 131076 | tf_op jit(solution)/shard_map/scatter-add | solution.py:87
  260.5 0.7 reshape.50
  261.2 41.9 %all-reduce.1 = (f32[]{:T(128)}, f32[]{:T(128)}) all-reduce(f32[]{:T(128)S(6)} %add.200, f32[]{:T(128)} %multiply_reduce_fusion.2), channel_id=1, replica_groups=mesh['tm'=8,'cal'=4] {'tm','cal'}, use_global_device_ids=true, to_apply=%region_3.0 | all-reduce | flops 2 | bytes 16 | tf_op jit(solution)/shard_map/psum | solution.py:110
  305.1 0.7 multiply_reduce_fusion.7
  307.1 0.9 constant_dynamic-slice_fusion.3
  308.0 30.1 %psum.37 = f32[2,4096]{1,0:T(2,128)S(1)} all-reduce(f32[2,4096]{1,0:T(2,128)S(1)} %constant_dynamic-slice_fusion.3), channel_id=1, replica_groups=mesh['tm'=8,'cal'=4] {'tm'}, use_global_device_ids=true, to_apply=%region_18.19 | all-reduce | flops 8192 | bytes 65536 | tf_op jit(solution)/shard_map/psum | solution.py:112
  338.1 0.6 multiply_reduce_fusion.3
  339.4 6.3 %psum.38 = f32[]{:T(128)} all-reduce(f32[]{:T(128)S(6)} %add.209), channel_id=1, replica_groups=mesh['tm'=8,'cal'=4] {'cal'}, use_global_device_ids=true, to_apply=%region_22.23 | all-reduce | flops 1 | bytes 8 | tf_op jit(solution)/shard_map/psum | solution.py:124
  345.7 22.7 %psum.39 = f32[]{:T(128)} all-reduce(f32[]{:T(128)} %psum.38), channel_id=1, replica_groups=mesh['tm'=8,'cal'=4] {'tm'}, use_global_device_ids=true, to_apply=%region_23.24 | all-reduce | flops 1 | bytes 8 | tf_op jit(solution)/shard_map/psum | solution.py:124
  370.9 0.6 multiply_add_fusion.1
  (152 shorter events, 38.1 us)
Async XLA Ops:
  7.2 3.9 %copy-start.4 = (f32[2,4096]{1,0:T(2,128)S(1)}, f32[2,4096]{1,0:T(2,128)}, u32[]{:S(2)}) copy-start(f32[2,4096]{1,0:T(2,128)} %param.33) | copy-start | bytes 98308
  7.2 299.9 %all-reduce.4.cloned.1.call-start = ((), (), s32[]{:S(2)}) async-start(), calls=%async_computation | async-start | bytes 262144
  7.2 106.4 %collective-permute-start = (f32[3,3]{1,0:T(4,128)}, f32[3,3]{1,0:T(4,128)S(1)}, u32[]{:S(2)}, u32[]{:S(2)}) collective-permute-start(f32[3,3]{1,0:T(4,128)} %bitcast.110), channel_id=1, source_target_pairs={{1,0},{2,1},{3,2},{4,3},{5,4},{6,5},{7,6},{8,7},{9,8},{10,9},{11,1... | collective-permute-start | bytes 116 | tf_op jit(solution)/shard_map/ppermute | solution.py:11
  10.1 6.4 %copy-start.3 = (f32[3,128,128]{2,1,0:T(8,128)S(1)}, f32[3,128,128]{2,1,0:T(8,128)}, u32[]{:S(2)}) copy-start(f32[3,128,128]{2,1,0:T(8,128)} %param.20) | copy-start | bytes 589828
  16.5 0.7 copy-start.12
  16.5 1.3 copy-start.13
  16.5 1.9 copy-start.6
  19.0 90.5 %copy-start = (f32[5,128,128]{2,1,0:T(8,128)S(1)}, f32[5,128,128]{2,1,0:T(8,128)}, u32[]{:S(2)}) copy-start(f32[5,128,128]{2,1,0:T(8,128)} %param.19) | copy-start | bytes 983044
  19.0 90.5 %copy-start.10 = (f32[5,128]{1,0:T(8,128)S(1)}, f32[5,128]{1,0:T(8,128)}, u32[]{:S(2)}) copy-start(f32[5,128]{1,0:T(8,128)} %param.31) | copy-start | bytes 7684
  109.5 0.8 copy-start.9
  109.6 2.8 copy-start.17
  109.6 4.0 %copy-start.14 = (f32[3,128]{1,0:T(4,128)S(1)}, f32[3,128]{1,0:T(4,128)}, u32[]{:S(2)}) copy-start(f32[3,128]{1,0:T(4,128)} %param.32) | copy-start | bytes 4612
  113.6 31.7 %copy-start.1 = (s32[128,128]{1,0:T(8,128)S(1)}, s32[128,128]{1,0:T(8,128)}, u32[]{:S(2)}) copy-start(s32[128,128]{1,0:T(8,128)} %param.26) | copy-start | bytes 196612
  113.6 31.7 %copy-start.2 = (s32[128,128]{1,0:T(8,128)S(1)}, s32[128,128]{1,0:T(8,128)}, u32[]{:S(2)}) copy-start(s32[128,128]{1,0:T(8,128)} %param.25) | copy-start | bytes 196612
  113.7 31.7 %copy-start.7 = (f32[128,128]{1,0:T(8,128)S(1)}, f32[128,128]{1,0:T(8,128)}, u32[]{:S(2)}) copy-start(f32[128,128]{1,0:T(8,128)} %param.22) | copy-start | bytes 196612
  113.7 31.7 %copy-start.8 = (f32[128,128]{1,0:T(8,128)S(1)}, f32[128,128]{1,0:T(8,128)}, u32[]{:S(2)}) copy-start(f32[128,128]{1,0:T(8,128)} %param.23) | copy-start | bytes 196612
  113.7 31.7 %copy-start.16 = (s32[128]{0:T(128)S(1)}, s32[128]{0:T(128)}, u32[]{:S(2)}) copy-start(s32[128]{0:T(128)} %param.27) | copy-start | bytes 1540
  172.4 132.7 %collective-permute-start.1 = (f32[3,3]{1,0:T(4,128)S(1)}, f32[3,3]{1,0:T(4,128)S(1)}, u32[]{:S(2)}, u32[]{:S(2)}) collective-permute-start(f32[3,3]{1,0:T(4,128)S(1)} %slice.14), channel_id=1, source_target_pairs={{0,1},{1,2},{2,3},{3,4},{4,5},{5,6},{6,7},{7,8},{8,9},{9,10},{10,1... | collective-permute-start | bytes 116 | tf_op jit(solution)/shard_map/ppermute | solution.py:11
  305.0 66.5 %copy-start.11 = (f32[5,128]{1,0:T(8,128)}, f32[5,128]{1,0:T(8,128)S(1)}, u32[]{:S(2)}) copy-start(f32[5,128]{1,0:T(8,128)S(1)} %get-tuple-element.349) | copy-start | bytes 7684
  305.7 65.8 %copy-start.15 = (f32[3,128]{1,0:T(4,128)}, f32[3,128]{1,0:T(4,128)S(1)}, u32[]{:S(2)}) copy-start(f32[3,128]{1,0:T(4,128)S(1)} %get-tuple-element.347) | copy-start | bytes 4612
  338.8 32.8 %copy-start.5 = (f32[2,4096]{1,0:T(2,128)}, f32[2,4096]{1,0:T(2,128)S(1)}, u32[]{:S(2)}) copy-start(f32[2,4096]{1,0:T(2,128)S(1)} %get-tuple-element.345) | copy-start | bytes 98308
Sparse Core Ops, SparseCore 0:
  261.3 33.1 all-reduce.3
